TPU v7x, 32 devices: a whole 2x2x4 slice. The times are simulated.
32 devices in a mesh: mol: 2 (over x), occ: 16 (over z, y, core).
Axes of the slice: x: 2, y: 2, z: 4, core: 2. Of those that a mesh axis runs over, the one named last changes fastest.
Arguments:
- integrals: bfloat16 [512, 128, 2048], P(('mol', 'occ')), parts along dimension 0, may hold values from -6 to 6
- orbitals: bfloat16 [4096, 1536], P('mol'), parts along dimension 0
- occ_energy: float32 [256], P('mol'), parts along dimension 0, may hold values from -2 to -0.3
- vir_energy: float32 [3072], P('mol'), parts along dimension 0, may hold values from 0.1 to 3
- owner: int32 [16], P('mol'), parts along dimension 0, may hold values from 0 to 127
- vblock: int32 [16], P('mol'), parts along dimension 0, may hold values from 0 to 7
Outputs:
- factors: bfloat16 [512, 128, 1536], P('mol', 'occ'), parts along dimension 0
- pair_energy: float32 [256, 8], P(('mol', 'occ')), parts along dimension 0
There are 2 independent parts, one for each index of `mol`. A program takes and returns all parts, laid end to end along the dimension named above; each array names one. Nothing has to cross between parts.
Inputs may be any that keep to these rules, and one draw needn't show every extreme that they name: `owner`: each step names one occupied orbital and one virtual block; steps may repeat.
All inputs are finite; a program needn't handle non-finite values.
Results may differ from a plain program's by a relative error of at most 0.001.
Values may be sent and summed in bfloat16 or wider, within the bound.
No kernel may reach another device: no remote copies, remote signals or barrier semaphores. Data moves between devices by JAX's collectives and lax.ppermute only.
A program may use at most 128 MiB of HBM per device.

v0:
```python
import jax
import jax.numpy as jnp
from jax import lax
from jax.sharding import PartitionSpec as P

VBLK = 192


def from_root(x, axis, root):
    mine = lax.axis_index(axis) == root
    return lax.psum(jnp.where(mine, x, jnp.zeros_like(x)), axis)


def pick_block(factors, orbital_j, block_id):
    local_count = factors.shape[1]
    row = orbital_j % local_count
    piece = lax.dynamic_slice(
        factors, (jnp.int32(0), row, block_id * VBLK), (factors.shape[0], 1, VBLK)
    )
    return (piece[:, 0, :], orbital_j // local_count)


def pair_column(factors, block, occ_here, occ_energy, vir_energy, orbital_j, block_id):
    coulomb = lax.dot_general(
        factors, block, (((0,), (0,)), ((), ())), preferred_element_type=jnp.float32
    )
    vir_block = lax.dynamic_slice(vir_energy, (block_id * VBLK,), (VBLK,))
    occ_j = occ_energy[orbital_j]
    denom = vir_energy[None, :, None] + vir_block[None, None, :] - occ_here[:, None, None] - occ_j
    scale = 1.0 / (factors.shape[0] * vir_energy.shape[0] * VBLK)
    return -jnp.sum(coulomb * coulomb / denom, axis=(1, 2)) * scale


def per_device(integrals, orbitals, occ_energy, vir_energy, owner, vblock):
    aux_here, occ_total, basis_count = integrals.shape
    step_count = owner.shape[0]
    flat = integrals.reshape(aux_here * occ_total, basis_count)
    product = jnp.dot(flat, orbitals, preferred_element_type=jnp.float32).astype(jnp.bfloat16)
    product = product.reshape(aux_here, occ_total, orbitals.shape[1])
    factors = lax.all_to_all(product, "occ", split_axis=1, concat_axis=0, tiled=True)
    local_count = factors.shape[1]
    occ_here = lax.dynamic_slice(occ_energy, (lax.axis_index("occ") * local_count,), (local_count,))
    energies = jnp.zeros((local_count, step_count), jnp.float32)

    def step_body(step, energies):
        orbital_j = owner[step]
        block_id = vblock[step]
        piece, root = pick_block(factors, orbital_j, block_id)
        block = from_root(piece, "occ", root)
        column = pair_column(factors, block, occ_here, occ_energy, vir_energy, orbital_j, block_id)
        return lax.dynamic_update_slice(energies, column[:, None], (jnp.int32(0), step))

    energies = lax.fori_loop(0, step_count, step_body, energies)
    return (factors, energies)


def solution(mesh):
    placed = (P(("mol", "occ"), None, None), P("mol", None), P("mol"), P("mol"), P("mol"), P("mol"))
    return jax.shard_map(
        per_device,
        mesh=mesh,
        in_specs=placed,
        out_specs=(P("mol", "occ", None), P(("mol", "occ"), None)),
        check_vma=False,
    )
```

profile of v0, /device:TPU:0, one launch (start us, length us, event | category | flops | bytes accessed | tf_op | source)
XLA Modules:
  0.0 991.6 jit_solution(14299061636335354797)
XLA Ops:
  7.2 17.3 %convolution_convert_fusion = bf16[2048,1536]{1,0:T(8,128)(2,1)S(1)} fusion(bf16[2048,2048]{1,0:T(8,128)(2,1)} %bitcast.42, bf16[2048,1536]{1,0:T(8,128)(2,1)} %param.9), kind=kOutput, calls=%fused_computation.6 | convolution fusion | flops 12888047616 | bytes 20971520 | tf_op jit(solution)/shard_map/dot_general | solution.py:38
  24.4 6.2 copy.13
  30.6 7.6 all-to-all-start
  38.3 114.1 %all-to-all-done = bf16[16,128,1536]{2,0,1:T(8,128)(2,1)} async-done(((bf16[16,128,1536]{2,0,1:T(8,128)(2,1)}), bf16[16,128,1536]{2,0,1:T(8,128)(2,1)}, u32[]{:S(2)}, u32[]{:S(2)}) %all-to-all-start) | async-done | bytes 6291488 | tf_op jit(solution)/shard_map/all_to_all | solution.py:40
  152.4 9.6 copy.14
  162.0 9.1 copy.15
  171.1 812.9 %while.15 = (s32[]{:T(128)}, f32[8,8]{0,1:T(8,128)S(1)}, s32[8]{0:T(128)S(1)}, s32[8]{0:T(128)S(1)}, bf16[256,8,1536]{0,2,1:T(8,128)(2,1)}, /*index=5*/f32[1536]...) while((s32[]{:T(128)}, f32[8,8]{0,1:T(8,128)S(1)}, ...), condition=%wide.region_3.4_spmd, body=%wide.region_0.3_spmd.sunk | while | flops 1220149248 | bytes 9544719 | solution.py:53
  171.2 0.7 dynamic_slice.61
  174.4 0.6 dynamic_slice.63
  175.6 1.6 select_bitcast_fusion.2
  177.3 0.1 broadcast_add_fusion.2
  178.7 0.6 dynamic_slice.62
  179.3 108.6 %all-reduce.2.cloned.1.call-done = bf16[256,192]{0,1:T(8,128)(2,1)} async-done(((bf16[256,192]{0,1:T(8,128)(2,1)}), bf16[256,192]{0,1:T(8,128)(2,1)}) %all-reduce.2.cloned.1.call-update) | async-done | bytes 98320 | tf_op jit(solution)/shard_map/while/body/eval_jaxpr/psum | solution.py:11
  287.9 6.2 fusion.10
  294.2 0.7 dynamic_slice.61
  297.3 0.6 dynamic_slice.63
  298.6 1.6 select_bitcast_fusion.2
  300.3 0.1 broadcast_add_fusion.2
  301.6 0.6 dynamic_slice.62
  302.3 84.2 %all-reduce.2.cloned.1.call-done = bf16[256,192]{0,1:T(8,128)(2,1)} async-done(((bf16[256,192]{0,1:T(8,128)(2,1)}), bf16[256,192]{0,1:T(8,128)(2,1)}) %all-reduce.2.cloned.1.call-update) | async-done | bytes 98320 | tf_op jit(solution)/shard_map/while/body/eval_jaxpr/psum | solution.py:11
  386.5 6.1 fusion.10
  392.7 0.7 dynamic_slice.61
  395.9 0.6 dynamic_slice.63
  397.2 1.6 select_bitcast_fusion.2
  398.8 0.1 broadcast_add_fusion.2
  400.2 0.6 dynamic_slice.62
  400.9 84.2 %all-reduce.2.cloned.1.call-done = bf16[256,192]{0,1:T(8,128)(2,1)} async-done(((bf16[256,192]{0,1:T(8,128)(2,1)}), bf16[256,192]{0,1:T(8,128)(2,1)}) %all-reduce.2.cloned.1.call-update) | async-done | bytes 98320 | tf_op jit(solution)/shard_map/while/body/eval_jaxpr/psum | solution.py:11
  485.1 6.1 fusion.10
  491.3 0.7 dynamic_slice.61
  494.5 0.6 dynamic_slice.63
  495.7 1.6 select_bitcast_fusion.2
  497.4 0.1 broadcast_add_fusion.2
  498.8 0.6 dynamic_slice.62
  499.5 84.2 %all-reduce.2.cloned.1.call-done = bf16[256,192]{0,1:T(8,128)(2,1)} async-done(((bf16[256,192]{0,1:T(8,128)(2,1)}), bf16[256,192]{0,1:T(8,128)(2,1)}) %all-reduce.2.cloned.1.call-update) | async-done | bytes 98320 | tf_op jit(solution)/shard_map/while/body/eval_jaxpr/psum | solution.py:11
  583.6 6.1 fusion.10
  589.9 0.7 dynamic_slice.61
  593.0 0.6 dynamic_slice.63
  594.3 1.6 select_bitcast_fusion.2
  596.0 0.1 broadcast_add_fusion.2
  597.4 0.6 dynamic_slice.62
  598.0 84.2 %all-reduce.2.cloned.1.call-done = bf16[256,192]{0,1:T(8,128)(2,1)} async-done(((bf16[256,192]{0,1:T(8,128)(2,1)}), bf16[256,192]{0,1:T(8,128)(2,1)}) %all-reduce.2.cloned.1.call-update) | async-done | bytes 98320 | tf_op jit(solution)/shard_map/while/body/eval_jaxpr/psum | solution.py:11
  682.2 6.1 fusion.10
  688.4 0.7 dynamic_slice.61
  691.6 0.6 dynamic_slice.63
  692.9 1.6 select_bitcast_fusion.2
  694.5 0.1 broadcast_add_fusion.2
  695.9 0.6 dynamic_slice.62
  696.6 84.2 %all-reduce.2.cloned.1.call-done = bf16[256,192]{0,1:T(8,128)(2,1)} async-done(((bf16[256,192]{0,1:T(8,128)(2,1)}), bf16[256,192]{0,1:T(8,128)(2,1)}) %all-reduce.2.cloned.1.call-update) | async-done | bytes 98320 | tf_op jit(solution)/shard_map/while/body/eval_jaxpr/psum | solution.py:11
  780.8 6.1 fusion.10
  787.0 0.7 dynamic_slice.61
  790.2 0.6 dynamic_slice.63
  791.4 1.6 select_bitcast_fusion.2
  793.1 0.1 broadcast_add_fusion.2
  794.5 0.6 dynamic_slice.62
  795.1 84.2 %all-reduce.2.cloned.1.call-done = bf16[256,192]{0,1:T(8,128)(2,1)} async-done(((bf16[256,192]{0,1:T(8,128)(2,1)}), bf16[256,192]{0,1:T(8,128)(2,1)}) %all-reduce.2.cloned.1.call-update) | async-done | bytes 98320 | tf_op jit(solution)/shard_map/while/body/eval_jaxpr/psum | solution.py:11
  879.3 6.1 fusion.10
  885.6 0.7 dynamic_slice.61
  888.7 0.6 dynamic_slice.63
  890.0 1.6 select_bitcast_fusion.2
  891.7 0.1 broadcast_add_fusion.2
  893.1 0.6 dynamic_slice.62
  893.7 84.2 %all-reduce.2.cloned.1.call-done = bf16[256,192]{0,1:T(8,128)(2,1)} async-done(((bf16[256,192]{0,1:T(8,128)(2,1)}), bf16[256,192]{0,1:T(8,128)(2,1)}) %all-reduce.2.cloned.1.call-update) | async-done | bytes 98320 | tf_op jit(solution)/shard_map/while/body/eval_jaxpr/psum | solution.py:11
  977.9 6.1 fusion.10
  984.1 0.7 copy.16
  (50 shorter events, 1.5 us)
Async XLA Ops:
  30.6 7.6 copy-start.3
  30.6 121.8 %all-to-all-start = ((bf16[16,128,1536]{2,0,1:T(8,128)(2,1)}), bf16[16,128,1536]{2,0,1:T(8,128)(2,1)}, u32[]{:S(2)}, u32[]{:S(2)}) async-start(bf16[16,128,1536]{2,0,1:T(8,128)(2,1)} %copy.13), calls=%async_computation | async-start | bytes 12582912 | tf_op jit(solution)/shard_map/all_to_all | solution.py:40
  162.0 9.1 copy-start
  162.0 9.1 copy-start.1
  162.0 9.1 copy-start.2
  171.2 116.8 %all-reduce.2.cloned.1.call-start = ((), (), s32[]{:S(2)}) async-start(), calls=%async_computation.1 | async-start | bytes 196608 | tf_op jit(solution)/shard_map/while/body/eval_jaxpr/psum | solution.py:11
  294.1 92.4 %all-reduce.2.cloned.1.call-start = ((), (), s32[]{:S(2)}) async-start(), calls=%async_computation.1 | async-start | bytes 196608 | tf_op jit(solution)/shard_map/while/body/eval_jaxpr/psum | solution.py:11
  392.7 92.4 %all-reduce.2.cloned.1.call-start = ((), (), s32[]{:S(2)}) async-start(), calls=%async_computation.1 | async-start | bytes 196608 | tf_op jit(solution)/shard_map/while/body/eval_jaxpr/psum | solution.py:11
  491.3 92.4 %all-reduce.2.cloned.1.call-start = ((), (), s32[]{:S(2)}) async-start(), calls=%async_computation.1 | async-start | bytes 196608 | tf_op jit(solution)/shard_map/while/body/eval_jaxpr/psum | solution.py:11
  589.8 92.4 %all-reduce.2.cloned.1.call-start = ((), (), s32[]{:S(2)}) async-start(), calls=%async_computation.1 | async-start | bytes 196608 | tf_op jit(solution)/shard_map/while/body/eval_jaxpr/psum | solution.py:11
  688.4 92.4 %all-reduce.2.cloned.1.call-start = ((), (), s32[]{:S(2)}) async-start(), calls=%async_computation.1 | async-start | bytes 196608 | tf_op jit(solution)/shard_map/while/body/eval_jaxpr/psum | solution.py:11
  787.0 92.4 %all-reduce.2.cloned.1.call-start = ((), (), s32[]{:S(2)}) async-start(), calls=%async_computation.1 | async-start | bytes 196608 | tf_op jit(solution)/shard_map/while/body/eval_jaxpr/psum | solution.py:11
  885.5 92.4 %all-reduce.2.cloned.1.call-start = ((), (), s32[]{:S(2)}) async-start(), calls=%async_computation.1 | async-start | bytes 196608 | tf_op jit(solution)/shard_map/while/body/eval_jaxpr/psum | solution.py:11
Sparse Core Ops, SparseCore 0:
  177.3 110.5 all-reduce.1
  300.3 86.1 all-reduce.1
  398.9 86.1 all-reduce.1
  497.5 86.1 all-reduce.1
  596.0 86.1 all-reduce.1
  694.6 86.1 all-reduce.1
  793.1 86.1 all-reduce.1
  891.7 86.1 all-reduce.1
where the time goes:
time: 993 us; the launch traced here: 992 us
  waiting for transfers between devices  812 us (82%)
  matrix products  66.4 us (7%)
  local copies, waits for them, and re-layouts  41.6 us (4%)
  loops' own time  35.7 us (4%)
  between operations  14.1 us (1%)
  other arithmetic  13.8 us (1%)
    psum x8, waiting for transfers between devices, from_root(): return lax.psum(jnp.where(mine, x, jnp.zeros_like(x)), axis)  698 us
    all_to_all x1, waiting for transfers between devices, per_device(): lax.all_to_all(product, 'occ', split_axis=1, concat_axis=0, tiled=True)  114 us
    dot_general x8, matrix products, pair_column(): lax.dot_general(factors, block, (((0,), (0,)), ((), ())), preferred_eleme...  49.2 us
    another operation x1, loops' own time, per_device(): energies = lax.fori_loop(0, step_count, step_body, energies)  35.7 us
  transfers between devices with their start and end apart: 9, of which 9 were waited for; matrix products, arithmetic and copies ran while one was open for 1% of the time, Pallas kernels for 0%

commit v1 on v0

--- a/solution.py
+++ b/solution.py
@@ -8,7 +8,7 @@
 
 def from_root(x, axis, root):
     mine = lax.axis_index(axis) == root
-    return lax.psum(jnp.where(mine, x, jnp.zeros_like(x)), axis)
+    return jnp.sum(lax.all_gather(jnp.where(mine, x, jnp.zeros_like(x)), axis), axis=0)
 
 
 def pick_block(factors, orbital_j, block_id):

time: 993 us -> 634 us (0.64)
  waiting for transfers between devices: 812 us -> 445 us
  other arithmetic: 13.8 us -> 30.1 us
    psum x8 -> x0, waiting for transfers between devices: 698 us -> none  [from_root(): return lax.psum(jnp.where(mine, x, jnp.zeros_like(x)), axis)]
    all_gather x0 -> x8, waiting for transfers between devices: none -> 330 us  [from_root(): lax.all_gather(jnp.where(mine, x, jnp.zeros_like(x)), axis)]
    reduce_sum x0 -> x8, other arithmetic: none -> 15.5 us  [from_root(): jnp.sum(lax.all_gather(jnp.where(mine, x, jnp.zeros_like(x)), axis), axis=0)]
where the time goes in v1:
time: 634 us; the launch traced here: 632 us
  waiting for transfers between devices  445 us (70%)
  matrix products  65.2 us (10%)
  loops' own time  35.7 us (6%)
  local copies, waits for them, and re-layouts  34.5 us (5%)
  other arithmetic  30.1 us (5%)
  between operations  14.1 us (2%)
  starting transfers between devices  7.9 us (1%)
    all_gather x8, waiting for transfers between devices, from_root(): lax.all_gather(jnp.where(mine, x, jnp.zeros_like(x)), axis)  330 us
    all_to_all x1, waiting for transfers between devices, per_device(): lax.all_to_all(product, 'occ', split_axis=1, concat_axis=0, tiled=True)  114 us
    dot_general x8, matrix products, pair_column(): lax.dot_general(factors, block, (((0,), (0,)), ((), ())), preferred_eleme...  48 us
    another operation x1, loops' own time, per_device(): energies = lax.fori_loop(0, step_count, step_body, energies)  35.7 us
    dot_general x1, matrix products, per_device(): jnp.dot(flat, orbitals, preferred_element_type=jnp.float32)  17.3 us
    reduce_sum x8, other arithmetic, from_root(): jnp.sum(lax.all_gather(jnp.where(mine, x, jnp.zeros_like(x)), axis), axis=0)  15.5 us
    select_n x8, other arithmetic, from_root(): jnp.where(mine, x, jnp.zeros_like(x))  13.4 us
  transfers between devices with their start and end apart: 9, of which 9 were waited for; matrix products, arithmetic and copies ran while one was open for 1% of the time, Pallas kernels for 0%

profile of v1, /device:TPU:0, one launch (start us, length us, event | category | flops | bytes accessed | tf_op | source)
XLA Modules:
  0.0 632.3 jit_solution(15171876444299976895)
XLA Ops:
  7.2 17.3 %convolution_convert_fusion = bf16[2048,1536]{1,0:T(8,128)(2,1)S(1)} fusion(bf16[2048,2048]{1,0:T(8,128)(2,1)} %bitcast.42, bf16[2048,1536]{1,0:T(8,128)(2,1)} %param.9), kind=kOutput, calls=%fused_computation.6 | convolution fusion | flops 12888047616 | bytes 20971520 | tf_op jit(solution)/shard_map/dot_general | solution.py:38
  24.4 6.2 copy.12
  30.6 7.6 %all-to-all-start = ((bf16[16,128,1536]{2,0,1:T(8,128)(2,1)}), bf16[16,128,1536]{2,0,1:T(8,128)(2,1)}, u32[]{:S(2)}, u32[]{:S(2)}) async-start(bf16[16,128,1536]{2,0,1:T(8,128)(2,1)} %copy.12), calls=%async_computation | async-start | bytes 12582912 | tf_op jit(solution)/shard_map/all_to_all | solution.py:40
  38.3 114.1 %all-to-all-done = bf16[16,128,1536]{2,0,1:T(8,128)(2,1)} async-done(((bf16[16,128,1536]{2,0,1:T(8,128)(2,1)}), bf16[16,128,1536]{2,0,1:T(8,128)(2,1)}, u32[]{:S(2)}, u32[]{:S(2)}) %all-to-all-start) | async-done | bytes 6291488 | tf_op jit(solution)/shard_map/all_to_all | solution.py:40
  152.4 6.9 %copy.13 = bf16[16,16,8,1536]{3,2,1,0:T(8,128)(2,1)S(1)} copy(bf16[16,16,8,1536]{3,1,2,0:T(8,128)(2,1)} %bitcast.10) | data formatting | bytes 12582912 | tf_op jit(solution)/shard_map/all_to_all | solution.py:40
  159.4 4.7 copy.14
  164.1 460.7 %while.15 = (s32[]{:T(128)}, f32[8,8]{0,1:T(8,128)S(1)}, s32[8]{0:T(128)S(1)}, s32[8]{0:T(128)S(1)}, bf16[256,8,1536]{2,0,1:T(8,128)(2,1)}, /*index=5*/f32[1536]...) while((s32[]{:T(128)}, f32[8,8]{0,1:T(8,128)S(1)}, ...), condition=%wide.region_3.4_spmd, body=%wide.region_0.3_spmd.sunk | while | flops 1220837376 | bytes 16196633 | solution.py:53
  164.1 0.7 dynamic_slice.61
  167.3 0.6 dynamic_slice.63
  168.6 1.7 dynamic-slice_select_fusion.2
  171.6 0.6 dynamic_slice.62
  172.3 62.9 %all-gather.5.cloned.1.call-done = bf16[4096,1,192]{2,0,1:T(8,128)(2,1)} async-done(((bf16[256,1,192]{2,0,1:T(8,128)(2,1)}), bf16[4096,1,192]{2,0,1:T(8,128)(2,1)}) %all-gather.5.cloned.1.call-update) | async-done | bytes 1572880 | tf_op jit(solution)/shard_map/while/body/eval_jaxpr/all_gather | solution.py:11
  235.2 1.9 reduce_sum.34
  237.2 6.0 fusion.10
  243.3 0.7 dynamic_slice.61
  246.4 0.6 dynamic_slice.63
  247.7 1.7 dynamic-slice_select_fusion.2
  250.7 0.6 dynamic_slice.62
  251.5 38.2 %all-gather.5.cloned.1.call-done = bf16[4096,1,192]{2,0,1:T(8,128)(2,1)} async-done(((bf16[256,1,192]{2,0,1:T(8,128)(2,1)}), bf16[4096,1,192]{2,0,1:T(8,128)(2,1)}) %all-gather.5.cloned.1.call-update) | async-done | bytes 1572880 | tf_op jit(solution)/shard_map/while/body/eval_jaxpr/all_gather | solution.py:11
  289.7 1.9 reduce_sum.34
  291.7 6.0 fusion.10
  297.8 0.7 dynamic_slice.61
  300.9 0.6 dynamic_slice.63
  302.2 1.7 dynamic-slice_select_fusion.2
  305.2 0.6 dynamic_slice.62
  306.0 38.2 %all-gather.5.cloned.1.call-done = bf16[4096,1,192]{2,0,1:T(8,128)(2,1)} async-done(((bf16[256,1,192]{2,0,1:T(8,128)(2,1)}), bf16[4096,1,192]{2,0,1:T(8,128)(2,1)}) %all-gather.5.cloned.1.call-update) | async-done | bytes 1572880 | tf_op jit(solution)/shard_map/while/body/eval_jaxpr/all_gather | solution.py:11
  344.2 1.9 reduce_sum.34
  346.2 6.0 fusion.10
  352.2 0.7 dynamic_slice.61
  355.4 0.6 dynamic_slice.63
  356.7 1.7 dynamic-slice_select_fusion.2
  359.7 0.6 dynamic_slice.62
  360.5 38.2 %all-gather.5.cloned.1.call-done = bf16[4096,1,192]{2,0,1:T(8,128)(2,1)} async-done(((bf16[256,1,192]{2,0,1:T(8,128)(2,1)}), bf16[4096,1,192]{2,0,1:T(8,128)(2,1)}) %all-gather.5.cloned.1.call-update) | async-done | bytes 1572880 | tf_op jit(solution)/shard_map/while/body/eval_jaxpr/all_gather | solution.py:11
  398.7 1.9 reduce_sum.34
  400.7 6.0 fusion.10
  406.8 0.7 dynamic_slice.61
  409.9 0.6 dynamic_slice.63
  411.2 1.7 dynamic-slice_select_fusion.2
  414.2 0.6 dynamic_slice.62
  415.0 38.2 %all-gather.5.cloned.1.call-done = bf16[4096,1,192]{2,0,1:T(8,128)(2,1)} async-done(((bf16[256,1,192]{2,0,1:T(8,128)(2,1)}), bf16[4096,1,192]{2,0,1:T(8,128)(2,1)}) %all-gather.5.cloned.1.call-update) | async-done | bytes 1572880 | tf_op jit(solution)/shard_map/while/body/eval_jaxpr/all_gather | solution.py:11
  453.2 1.9 reduce_sum.34
  455.2 6.0 fusion.10
  461.3 0.7 dynamic_slice.61
  464.4 0.6 dynamic_slice.63
  465.7 1.7 dynamic-slice_select_fusion.2
  468.7 0.6 dynamic_slice.62
  469.5 38.2 %all-gather.5.cloned.1.call-done = bf16[4096,1,192]{2,0,1:T(8,128)(2,1)} async-done(((bf16[256,1,192]{2,0,1:T(8,128)(2,1)}), bf16[4096,1,192]{2,0,1:T(8,128)(2,1)}) %all-gather.5.cloned.1.call-update) | async-done | bytes 1572880 | tf_op jit(solution)/shard_map/while/body/eval_jaxpr/all_gather | solution.py:11
  507.7 1.9 reduce_sum.34
  509.7 6.0 fusion.10
  515.8 0.7 dynamic_slice.61
  518.9 0.6 dynamic_slice.63
  520.2 1.7 dynamic-slice_select_fusion.2
  523.2 0.6 dynamic_slice.62
  524.0 38.2 %all-gather.5.cloned.1.call-done = bf16[4096,1,192]{2,0,1:T(8,128)(2,1)} async-done(((bf16[256,1,192]{2,0,1:T(8,128)(2,1)}), bf16[4096,1,192]{2,0,1:T(8,128)(2,1)}) %all-gather.5.cloned.1.call-update) | async-done | bytes 1572880 | tf_op jit(solution)/shard_map/while/body/eval_jaxpr/all_gather | solution.py:11
  562.3 1.9 reduce_sum.34
  564.2 6.0 fusion.10
  570.3 0.7 dynamic_slice.61
  573.4 0.6 dynamic_slice.63
  574.7 1.7 dynamic-slice_select_fusion.2
  577.7 0.6 dynamic_slice.62
  578.5 38.2 %all-gather.5.cloned.1.call-done = bf16[4096,1,192]{2,0,1:T(8,128)(2,1)} async-done(((bf16[256,1,192]{2,0,1:T(8,128)(2,1)}), bf16[4096,1,192]{2,0,1:T(8,128)(2,1)}) %all-gather.5.cloned.1.call-update) | async-done | bytes 1572880 | tf_op jit(solution)/shard_map/while/body/eval_jaxpr/all_gather | solution.py:11
  616.8 1.9 reduce_sum.34
  618.7 6.0 fusion.10
  624.7 0.7 copy.15
  (60 shorter events, 2.6 us)
Async XLA Ops:
  30.6 7.6 %copy-start.4 = (f32[128]{0:T(128)S(1)}, f32[128]{0:T(128)}, u32[]{:S(2)}) copy-start(f32[128]{0:T(128)} %param.10) | copy-start | bytes 1540
  30.6 121.8 %all-to-all-start = ((bf16[16,128,1536]{2,0,1:T(8,128)(2,1)}), bf16[16,128,1536]{2,0,1:T(8,128)(2,1)}, u32[]{:S(2)}, u32[]{:S(2)}) async-start(bf16[16,128,1536]{2,0,1:T(8,128)(2,1)} %copy.12), calls=%async_computation | async-start | bytes 12582912 | tf_op jit(solution)/shard_map/all_to_all | solution.py:40
  159.3 4.7 copy-start
  159.3 4.7 copy-start.1
  159.3 4.7 copy-start.2
  159.3 4.7 copy-start.3
  164.1 71.1 %all-gather.5.cloned.1.call-start = ((), (), s32[]{:S(2)}) async-start(), calls=%async_computation.1 | async-start | bytes 2228224 | tf_op jit(solution)/shard_map/while/body/eval_jaxpr/all_gather | solution.py:11
  243.2 46.5 %all-gather.5.cloned.1.call-start = ((), (), s32[]{:S(2)}) async-start(), calls=%async_computation.1 | async-start | bytes 2228224 | tf_op jit(solution)/shard_map/while/body/eval_jaxpr/all_gather | solution.py:11
  297.7 46.5 %all-gather.5.cloned.1.call-start = ((), (), s32[]{:S(2)}) async-start(), calls=%async_computation.1 | async-start | bytes 2228224 | tf_op jit(solution)/shard_map/while/body/eval_jaxpr/all_gather | solution.py:11
  352.2 46.5 %all-gather.5.cloned.1.call-start = ((), (), s32[]{:S(2)}) async-start(), calls=%async_computation.1 | async-start | bytes 2228224 | tf_op jit(solution)/shard_map/while/body/eval_jaxpr/all_gather | solution.py:11
  406.7 46.5 %all-gather.5.cloned.1.call-start = ((), (), s32[]{:S(2)}) async-start(), calls=%async_computation.1 | async-start | bytes 2228224 | tf_op jit(solution)/shard_map/while/body/eval_jaxpr/all_gather | solution.py:11
  461.2 46.5 %all-gather.5.cloned.1.call-start = ((), (), s32[]{:S(2)}) async-start(), calls=%async_computation.1 | async-start | bytes 2228224 | tf_op jit(solution)/shard_map/while/body/eval_jaxpr/all_gather | solution.py:11
  515.7 46.5 %all-gather.5.cloned.1.call-start = ((), (), s32[]{:S(2)}) async-start(), calls=%async_computation.1 | async-start | bytes 2228224 | tf_op jit(solution)/shard_map/while/body/eval_jaxpr/all_gather | solution.py:11
  570.2 46.5 %all-gather.5.cloned.1.call-start = ((), (), s32[]{:S(2)}) async-start(), calls=%async_computation.1 | async-start | bytes 2228224 | tf_op jit(solution)/shard_map/while/body/eval_jaxpr/all_gather | solution.py:11
Sparse Core Ops, SparseCore 0:
  170.4 64.8 all-gather.4
  249.5 40.1 all-gather.4
  304.0 40.1 all-gather.4
  358.5 40.1 all-gather.4
  413.0 40.1 all-gather.4
  467.5 40.1 all-gather.4
  522.0 40.1 all-gather.4
  576.5 40.1 all-gather.4
